TPU v7x, 32 devices: a whole 2x2x4 slice. The times are simulated.
32 devices in a mesh: dp: 8 (over y, x, core), space: 4 (over z).
Axes of the slice: x: 2, y: 2, z: 4, core: 2. Of those that a mesh axis runs over, the one named last changes fastest.
Arguments:
- volume: bfloat16 [8, 32, 8, 16, 128], P('dp', None, 'space')
- out_grad: bfloat16 [8, 32, 8, 16, 128], P('dp', None, 'space'), may hold values from -0.016479492 to 0.016479492
- kernel: bfloat16 [32, 864], replicated, may hold values from -0.21875 to 0.21875
- sample_idx: int32 [8, 4096], P('dp', 'space'), may hold values from 0 to 4095
- a_inverse: float32 [864, 864], P('space')
- g_inverse: float32 [32, 32], replicated
Outputs:
- conv_out: bfloat16 [8, 32, 8, 16, 128], P('dp', None, 'space')
- a_factor: float32 [864, 864], P('dp', 'space')
- g_factor: float32 [32, 32], replicated
- pre_grad: float32 [32, 864], replicated
Inputs may be any that keep to these rules, and one draw needn't show every extreme that they name: `sample_idx`: column s of a sample's row names a cell of slab s // 1024, as the number z * 16 * 128 + y * 128 + x counted within that slab of 2 planes.
All inputs are finite; a program needn't handle non-finite values.
Results may differ from a plain program's by a relative error of at most 0.0085.
Values may be sent and summed in bfloat16 or wider, within the bound.
No kernel may reach another device: no remote copies, remote signals or barrier semaphores. Data moves between devices by JAX's collectives and lax.ppermute only.
A program may use at most 128 MiB of HBM per device.

v0:
```python
import jax
import jax.numpy as jnp
from jax import lax
from jax.sharding import PartitionSpec as P


def padded_2(cells, sides, width):
    for axis, dim in sides:
        count = lax.axis_size(axis)
        ends = count - 1
        head = lax.slice_in_dim(cells, 0, width, axis=dim)
        tail = lax.slice_in_dim(cells, cells.shape[dim] - width, cells.shape[dim], axis=dim)
        cells = jnp.concatenate(
            [
                lax.ppermute(tail, axis, [(i, (i + 1) % count) for i in range(ends)]),
                cells,
                lax.ppermute(head, axis, [((i + 1) % count, i) for i in range(ends)]),
            ],
            axis=dim,
        )
    return cells


def on_device(volume, out_grad, kernel, sample_idx, a_inverse, g_inverse):
    highest = lax.Precision.HIGHEST
    f32 = jnp.float32
    channels = volume.shape[1]
    planes = volume.shape[2]
    y_cells = volume.shape[3]
    x_cells = volume.shape[4]
    cells = planes * y_cells * x_cells
    patch = kernel.shape[1]
    n_dp = lax.axis_size("dp")
    n_sp = lax.axis_size("space")
    contract_cells = (((1,), (1,)), ((), ()))
    block = padded_2(volume, (("space", 2),), 1)
    padded = jnp.pad(block[0], ((0, 0), (0, 0), (1, 1), (1, 1)))
    taps = [
        padded[:, dz : dz + planes, dy : dy + y_cells, dx : dx + x_cells]
        for dz in range(3)
        for dy in range(3)
        for dx in range(3)
    ]
    patches_t = jnp.stack(taps, axis=1).reshape(patch, cells)
    grad_flat = out_grad[0].reshape(channels, cells)
    forward = jnp.dot(kernel, patches_t, preferred_element_type=f32)
    conv_out = forward.astype(jnp.bfloat16).reshape(1, channels, planes, y_cells, x_cells)
    grad_w = lax.dot_general(grad_flat, patches_t, contract_cells, preferred_element_type=f32)
    g_part = lax.dot_general(grad_flat, grad_flat, contract_cells, preferred_element_type=f32)
    cell_ids = sample_idx[0]
    counts = jnp.sum(
        (cell_ids[:, None] == jnp.arange(cells, dtype=jnp.int32)[None, :]).astype(f32), axis=0
    )
    weighted = patches_t.astype(f32) * counts[None, :]
    high = weighted.astype(jnp.bfloat16)
    low = (weighted - high.astype(f32)).astype(jnp.bfloat16)
    total_samples = sample_idx.shape[1] * n_sp * n_dp
    a_part = (
        lax.dot_general(high, patches_t, contract_cells, preferred_element_type=f32)
        + lax.dot_general(low, patches_t, contract_cells, preferred_element_type=f32)
    ) / jnp.float32(total_samples)
    rows = patch // n_dp
    cols = patch // n_sp
    a_blocks = (
        a_part.astype(jnp.bfloat16)
        .reshape(n_dp, rows, n_sp, cols)
        .transpose(0, 2, 1, 3)
        .reshape(n_dp * n_sp, rows, cols)
    )
    a_factor = lax.psum_scatter(a_blocks, ("dp", "space"), scatter_dimension=0, tiled=True)
    a_factor = a_factor.reshape(rows, cols).astype(f32)
    both = lax.psum(jnp.concatenate([grad_w, g_part], axis=1), ("dp", "space"))
    grad_sum = both[:, :patch]
    g_factor = both[:, patch:]
    left = jnp.dot(g_inverse, grad_sum, precision=highest)
    own_rows = a_inverse.shape[0]
    left_rows = lax.dynamic_slice_in_dim(left, lax.axis_index("space") * own_rows, own_rows, axis=1)
    pre_grad = lax.psum(jnp.dot(left_rows, a_inverse, precision=highest), "space")
    return (conv_out, a_factor, g_factor, pre_grad)


def solution(mesh):
    placed = (
        P("dp", None, "space", None, None),
        P("dp", None, "space", None, None),
        P(),
        P("dp", "space"),
        P("space", None),
        P(),
    )
    return jax.shard_map(
        on_device,
        mesh=mesh,
        in_specs=placed,
        out_specs=(P("dp", None, "space", None, None), P("dp", "space"), P(), P()),
        check_vma=False,
    )
```

profile of v0, /device:TPU:0, one launch (start us, length us, event | category | flops | bytes accessed | tf_op | source)
XLA Modules:
  0.0 373.9 jit_solution(7109457592317233880)
XLA Ops:
  7.2 1.1 fusion.59
  8.3 4.9 %collective-permute-start = (bf16[1,32,1,16,128]{4,3,2,1,0:T(8,128)(2,1)S(1)}, bf16[1,32,1,16,128]{4,3,2,1,0:T(8,128)(2,1)S(1)}, u32[]{:S(2)}, u32[]{:S(2)}) collective-permute-start(bf16[1,32,1,16,128]{4,3,2,1,0:T(8,128)(2,1)S(1)} %get-tuple-element.6), channel_id=1, source_target_pairs={{0,1},{1,2},{2,3},{4,5},{5,6},{6,7},{8,9},{9,10},{10,11},{12,13},{... | collective-permute-start | bytes 393224 | tf_op jit(solution)/shard_map/ppermute | solution.py:15
  13.2 1.3 collective-permute-start.1
  14.5 3.4 convert_reduce_fusion
  17.9 1.1 reshape_squeeze.3
  19.0 1.3 convolution_bitcast_fusion.1
  20.3 1.0 maximum_bitcast_fusion
  24.4 0.2 fusion.39
  25.6 4.6 %copy.25 = bf16[32,27,2,16,128]{4,3,2,1,0:T(8,128)(2,1)} copy(bf16[32,27,2,16,128]{4,3,2,0,1:T(8,128)(2,1)S(1)} %fusion.49) | data formatting | bytes 14155776 | tf_op jit(solution)/shard_map/stack | solution.py:44
  30.2 0.7 copy-done.1
  30.8 12.0 %subtract_convert_fusion = (bf16[32,27,2,16,128]{4,3,2,0,1:T(8,128)(2,1)}, bf16[32,27,2,16,128]{4,3,2,0,1:T(8,128)(2,1)}) fusion(bf16[32,27,2,16,128]{4,3,2,0,1:T(8,128)(2,1)} %copy-done.1, f32[2,16,128]{2,1,0:T(8,128)S(1)} %bitcast.151), kind=kLoop, calls=%fused_computation.2 | loop fusion | flops 21233664 | bytes 21250048 | tf_op jit(solution)/shard_map/convert_element_type | solution.py:56
  42.9 7.1 %copy.26 = bf16[32,27,2,16,128]{4,3,2,1,0:T(8,128)(2,1)} copy(bf16[32,27,2,16,128]{4,3,2,0,1:T(8,128)(2,1)} %get-tuple-element.5) | data formatting | bytes 14155776 | tf_op jit(solution)/shard_map/convert_element_type | solution.py:55
  50.0 11.6 %convert_element_type.83 = bf16[864,4096]{1,0:T(8,128)(2,1)} reshape(bf16[32,27,2,16,128]{4,3,2,1,0:T(8,128)(2,1)} %copy.26) | data formatting | bytes 14155776 | tf_op jit(solution)/shard_map/convert_element_type | solution.py:55
  61.6 11.6 %reshape.94 = bf16[864,4096]{1,0:T(8,128)(2,1)} reshape(bf16[32,27,2,16,128]{4,3,2,1,0:T(8,128)(2,1)} %copy.25) | data formatting | bytes 14155776 | tf_op jit(solution)/shard_map/reshape | solution.py:44
  73.2 7.1 %copy.27 = bf16[32,27,2,16,128]{4,3,2,1,0:T(8,128)(2,1)} copy(bf16[32,27,2,16,128]{4,3,2,0,1:T(8,128)(2,1)} %get-tuple-element.4) | data formatting | bytes 14155776 | tf_op jit(solution)/shard_map/convert_element_type | solution.py:56
  80.3 11.6 %convert_element_type.86 = bf16[864,4096]{1,0:T(8,128)(2,1)} reshape(bf16[32,27,2,16,128]{4,3,2,1,0:T(8,128)(2,1)} %copy.27) | data formatting | bytes 14155776 | tf_op jit(solution)/shard_map/convert_element_type | solution.py:56
  91.9 12.9 %fusion.60 = f32[864,864]{1,0:T(8,128)} fusion(bf16[864,4096]{1,0:T(8,128)(2,1)} %convert_element_type.83, bf16[864,4096]{1,0:T(8,128)(2,1)} %reshape.94), kind=kOutput, calls=%fused_computation.98 | convolution fusion | flops 6115295232 | bytes 17141760 | tf_op jit(solution)/shard_map/dot_general | solution.py:59
  104.8 5.1 %convolution_bitcast_fusion = f32[32,864]{1,0:T(8,128)S(1)} fusion(bf16[864,4096]{1,0:T(8,128)(2,1)} %reshape.94, bf16[32,4096]{1,0:T(8,128)(2,1)S(1)} %reshape_squeeze.3), kind=kOutput, calls=%fused_computation.32 | convolution fusion | flops 226492416 | bytes 7450624 | tf_op jit(solution)/shard_map/dot_general | solution.py:48
  109.9 0.7 pad_maximum_fusion
  110.7 13.3 %multiply_convert_fusion = bf16[864,864]{1,0:T(8,128)(2,1)} fusion(f32[864,864]{1,0:T(8,128)} %fusion.60, bf16[864,4096]{1,0:T(8,128)(2,1)} %convert_element_type.86, bf16[864,4096]{1,0:T(8,128)(2,1)} %reshape.94), kind=kOutput, calls=%fused_computation.30 | convolution fusion | flops 6117534720 | bytes 18634752 | tf_op jit(solution)/shard_map/dot_general | solution.py:60
  124.0 4.6 %reshape.96 = bf16[8,108,4,216]{3,2,1,0:T(4,128)(2,1)S(1)} reshape(bf16[864,864]{1,0:T(8,128)(2,1)} %multiply_convert_fusion) | data formatting | bytes 2985984 | tf_op jit(solution)/shard_map/reshape | solution.py:66
  128.6 2.6 copy.28
  131.2 4.4 %fusion.1 = bf16[4,8,32,128]{3,1,2,0:T(8,128)(2,1)S(1)} fusion(bf16[32,864]{1,0:T(8,128)(2,1)S(1)} %copy-done.2, bf16[864,4096]{1,0:T(8,128)(2,1)} %reshape.94), kind=kOutput, calls=%fused_computation.31 | convolution fusion | flops 226623488 | bytes 7395328 | tf_op jit(solution)/shard_map/dot_general | solution.py:46
  135.6 0.8 copy.32
  136.3 97.5 %all-reduce.5.cloned.1.call-done = f32[32,896]{1,0:T(8,128)} async-done(((f32[32,896]{1,0:T(8,128)}), f32[32,896]{1,0:T(8,128)}) %all-reduce.5.cloned.1.call-update) | async-done | bytes 114704 | tf_op jit(solution)/shard_map/psum | solution.py:72
  233.8 1.1 fusion.54
  235.0 1.3 fusion.56
  236.3 1.4 slice.130
  237.7 92.0 %reduce-scatter.4.cloned.1.call-done = bf16[1,108,216]{1,2,0:T(8,128)(2,1)} async-done(((bf16[32,108,216]{1,2,0:T(8,128)(2,1)}), bf16[1,108,216]{1,2,0:T(8,128)(2,1)}) %reduce-scatter.4.cloned.1.call-update) | async-done | bytes 46672
  329.7 1.5 bitcast_convert_fusion
  331.2 34.7 %all-reduce.7.cloned.1.call-done = f32[32,864]{1,0:T(8,128)} async-done(((f32[32,864]{1,0:T(8,128)}), f32[32,864]{1,0:T(8,128)}) %all-reduce.7.cloned.1.call-update) | async-done | bytes 110608 | tf_op jit(solution)/shard_map/psum | solution.py:78
  365.9 1.6 copy.63
  (41 shorter events, 4.1 us)
Async XLA Ops:
  7.2 227.8 %copy-start = (f32[216,864]{1,0:T(8,128)S(1)}, f32[216,864]{1,0:T(8,128)}, u32[]{:S(2)}) copy-start(f32[216,864]{1,0:T(8,128)} %param.10) | copy-start | bytes 2239492
  7.2 226.7 %all-reduce.5.cloned.1.call-start = ((), (), s32[]{:S(2)}) async-start(), calls=%async_computation.1 | async-start | bytes 229376 | tf_op jit(solution)/shard_map/psum | solution.py:72
  8.3 12.0 %collective-permute-start = (bf16[1,32,1,16,128]{4,3,2,1,0:T(8,128)(2,1)S(1)}, bf16[1,32,1,16,128]{4,3,2,1,0:T(8,128)(2,1)S(1)}, u32[]{:S(2)}, u32[]{:S(2)}) collective-permute-start(bf16[1,32,1,16,128]{4,3,2,1,0:T(8,128)(2,1)S(1)} %get-tuple-element.6), channel_id=1, source_target_pairs={{0,1},{1,2},{2,3},{4,5},{5,6},{6,7},{8,9},{9,10},{10,11},{12,13},{... | collective-permute-start | bytes 393224 | tf_op jit(solution)/shard_map/ppermute | solution.py:15
  13.2 7.0 %collective-permute-start.1 = (bf16[1,32,1,16,128]{4,3,2,1,0:T(8,128)(2,1)S(1)}, bf16[1,32,1,16,128]{4,3,2,1,0:T(8,128)(2,1)S(1)}, u32[]{:S(2)}, u32[]{:S(2)}) collective-permute-start(bf16[1,32,1,16,128]{4,3,2,1,0:T(8,128)(2,1)S(1)} %get-tuple-element.7), channel_id=1, source_target_pairs={{1,0},{2,1},{3,2},{5,4},{6,5},{7,6},{9,8},{10,9},{11,10},{13,12},{... | collective-permute-start | bytes 393224 | tf_op jit(solution)/shard_map/ppermute | solution.py:17
  25.6 5.3 %copy-start.1 = (bf16[32,27,2,16,128]{4,3,2,0,1:T(8,128)(2,1)}, bf16[32,27,2,16,128]{4,3,2,0,1:T(8,128)(2,1)S(1)}, u32[]{:S(2)}) copy-start(bf16[32,27,2,16,128]{4,3,2,0,1:T(8,128)(2,1)S(1)} %fusion.49) | copy-start | bytes 21233668
  110.7 219.0 %reduce-scatter.4.cloned.1.call-start = ((), (), s32[]{:S(2)}) async-start(), calls=%async_computation.3 | async-start | bytes 1824768
  124.0 7.2 %copy-start.2 = (bf16[32,864]{1,0:T(8,128)(2,1)S(1)}, bf16[32,864]{1,0:T(8,128)(2,1)}, u32[]{:S(2)}) copy-start(bf16[32,864]{1,0:T(8,128)(2,1)} %param.8) | copy-start | bytes 165892
  128.5 105.3 %copy-start.3 = (f32[32,32]{1,0:T(8,128)S(1)}, f32[32,32]{1,0:T(8,128)}, u32[]{:S(2)}) copy-start(f32[32,32]{1,0:T(8,128)} %param.11) | copy-start | bytes 12292
  131.1 234.7 %all-reduce.7.cloned.1.call-start = ((), (), s32[]{:S(2)}) async-start(), calls=%async_computation.2 | async-start | bytes 229376 | tf_op jit(solution)/shard_map/psum | solution.py:78
Sparse Core Ops, SparseCore 0:
  110.8 123.0 all-reduce.4
  239.2 90.4 reduce-scatter.3
  332.7 33.1 all-reduce.6
where the time goes:
time: 375 us; the launch traced here: 374 us
  waiting for transfers between devices  224 us (60%)
  local copies, waits for them, and re-layouts  71.4 us (19%)
  matrix products  39.4 us (11%)
  other arithmetic  18.6 us (5%)
  between operations  14 us (4%)
  starting transfers between devices  6.35 us (2%)
    psum x1, waiting for transfers between devices, on_device(): both = lax.psum(jnp.concatenate([grad_w, g_part], axis=1), ('dp', 'space'))  97.5 us
    unnamed x4, waiting for transfers between devices  92 us
    psum x1, waiting for transfers between devices, on_device(): lax.psum(jnp.dot(left_rows, a_inverse, precision=highest), 'space')  34.7 us
    convert_element_type x2, local copies, waits for them, and re-layouts, on_device(): high = weighted.astype(jnp.bfloat16)  18.8 us
    convert_element_type x2, local copies, waits for them, and re-layouts, on_device(): low = (weighted - high.astype(f32)).astype(jnp.bfloat16)  18.6 us
    dot_general x1, matrix products, on_device(): lax.dot_general(low, patches_t, contract_cells, preferred_element_type=f32)  13.3 us
    dot_general x1, matrix products, on_device(): lax.dot_general(high, patches_t, contract_cells, preferred_element_type=f32)  12.9 us
    convert_element_type x1, other arithmetic, on_device(): low = (weighted - high.astype(f32)).astype(jnp.bfloat16)  12 us
  transfers between devices with their start and end apart: 5, of which 3 were waited for; matrix products, arithmetic and copies ran while one was open for 10% of the time, Pallas kernels for 0%

commit v1 on v0

--- a/solution.py
+++ b/solution.py
@@ -69,7 +69,7 @@
     )
     a_factor = lax.psum_scatter(a_blocks, ("dp", "space"), scatter_dimension=0, tiled=True)
     a_factor = a_factor.reshape(rows, cols).astype(f32)
-    both = lax.psum(jnp.concatenate([grad_w, g_part], axis=1), ("dp", "space"))
+    both = lax.psum(lax.psum(jnp.concatenate([grad_w, g_part], axis=1), "space"), "dp")
     grad_sum = both[:, :patch]
     g_factor = both[:, patch:]
     left = jnp.dot(g_inverse, grad_sum, precision=highest)

time: 375 us -> 239 us (0.64)
  waiting for transfers between devices: 224 us -> 86.2 us
    psum x1 -> x2, waiting for transfers between devices: 97.5 us -> 34 us  [the longest x1 29 us: on_device(): lax.psum(lax.psum(jnp.concatenate([grad_w, g_part], axis=1), 'space'), 'dp')]
    unnamed x4 -> x5, waiting for transfers between devices: 92 us -> 52.2 us
    psum x1, waiting for transfers between devices: 34.7 us -> 0.01 us  [on_device(): lax.psum(jnp.dot(left_rows, a_inverse, precision=highest), 'space')]
  transfers between devices with their start and end apart: 5 -> 6, of which waited for: 3 -> 3; matrix products, arithmetic and copies ran while one was open for 10% -> 29% of each run, Pallas kernels for 0% -> 0%
where the time goes in v1:
time: 239 us; the launch traced here: 237 us
  waiting for transfers between devices  86.2 us (36%)
  local copies, waits for them, and re-layouts  71.3 us (30%)
  matrix products  39.3 us (16%)
  other arithmetic  18.7 us (8%)
  between operations  15.4 us (6%)
  starting transfers between devices  6.39 us (3%)
    unnamed x5, waiting for transfers between devices  52.2 us
    psum x1, waiting for transfers between devices, on_device(): lax.psum(lax.psum(jnp.concatenate([grad_w, g_part], axis=1), 'space'), 'dp')  29 us
    convert_element_type x2, local copies, waits for them, and re-layouts, on_device(): high = weighted.astype(jnp.bfloat16)  18.8 us
    convert_element_type x2, local copies, waits for them, and re-layouts, on_device(): low = (weighted - high.astype(f32)).astype(jnp.bfloat16)  18.6 us
    dot_general x1, matrix products, on_device(): lax.dot_general(low, patches_t, contract_cells, preferred_element_type=f32)  13.2 us
    dot_general x1, matrix products, on_device(): lax.dot_general(high, patches_t, contract_cells, preferred_element_type=f32)  12.9 us
    convert_element_type x1, other arithmetic, on_device(): low = (weighted - high.astype(f32)).astype(jnp.bfloat16)  12.1 us
    reshape x1, local copies, waits for them, and re-layouts, on_device(): patches_t = jnp.stack(taps, axis=1).reshape(patch, cells)  11.6 us
  transfers between devices with their start and end apart: 6, of which 3 were waited for; matrix products, arithmetic and copies ran while one was open for 29% of the time, Pallas kernels for 0%

profile of v1, /device:TPU:0, one launch (start us, length us, event | category | flops | bytes accessed | tf_op | source)
XLA Modules:
  0.0 237.4 jit_solution(1246254837047836308)
XLA Ops:
  8.1 1.1 fusion.59
  9.1 4.9 %collective-permute-start = (bf16[1,32,1,16,128]{4,3,2,1,0:T(8,128)(2,1)S(1)}, bf16[1,32,1,16,128]{4,3,2,1,0:T(8,128)(2,1)S(1)}, u32[]{:S(2)}, u32[]{:S(2)}) collective-permute-start(bf16[1,32,1,16,128]{4,3,2,1,0:T(8,128)(2,1)S(1)} %get-tuple-element.6), channel_id=1, source_target_pairs={{0,1},{1,2},{2,3},{4,5},{5,6},{6,7},{8,9},{9,10},{10,11},{12,13},{... | collective-permute-start | bytes 393224 | tf_op jit(solution)/shard_map/ppermute | solution.py:15
  14.1 1.3 collective-permute-start.1
  15.4 3.4 %convert_reduce_fusion = f32[4096]{0:T(1024)S(1)} fusion(s32[1024]{0:T(1024)} %bitcast.152), kind=kLoop, calls=%fused_computation | loop fusion | flops 12578816 | bytes 20480 | tf_op jit(solution)/shard_map/reduce_sum | solution.py:51
  18.7 1.1 reshape_squeeze.3
  19.8 1.3 convolution_bitcast_fusion.1
  21.1 1.0 maximum_bitcast_fusion
  22.4 0.2 fusion.7
  26.4 4.5 %copy.25 = bf16[32,27,2,16,128]{4,3,2,1,0:T(8,128)(2,1)} copy(bf16[32,27,2,16,128]{4,3,2,0,1:T(8,128)(2,1)S(1)} %fusion.49) | data formatting | bytes 14155776 | tf_op jit(solution)/shard_map/stack | solution.py:44
  30.9 0.7 copy-done.1
  31.7 12.1 %subtract_convert_fusion = (bf16[32,27,2,16,128]{4,3,2,0,1:T(8,128)(2,1)}, bf16[32,27,2,16,128]{4,3,2,0,1:T(8,128)(2,1)}) fusion(bf16[32,27,2,16,128]{4,3,2,0,1:T(8,128)(2,1)} %copy-done.1, f32[2,16,128]{2,1,0:T(8,128)S(1)} %bitcast.151), kind=kLoop, calls=%fused_computation.2 | loop fusion | flops 21233664 | bytes 21250048 | tf_op jit(solution)/shard_map/convert_element_type | solution.py:56
  43.8 7.1 %copy.26 = bf16[32,27,2,16,128]{4,3,2,1,0:T(8,128)(2,1)} copy(bf16[32,27,2,16,128]{4,3,2,0,1:T(8,128)(2,1)} %get-tuple-element.5) | data formatting | bytes 14155776 | tf_op jit(solution)/shard_map/convert_element_type | solution.py:55
  51.0 11.6 %convert_element_type.83 = bf16[864,4096]{1,0:T(8,128)(2,1)} reshape(bf16[32,27,2,16,128]{4,3,2,1,0:T(8,128)(2,1)} %copy.26) | data formatting | bytes 14155776 | tf_op jit(solution)/shard_map/convert_element_type | solution.py:55
  62.6 11.6 %reshape.94 = bf16[864,4096]{1,0:T(8,128)(2,1)} reshape(bf16[32,27,2,16,128]{4,3,2,1,0:T(8,128)(2,1)} %copy.25) | data formatting | bytes 14155776 | tf_op jit(solution)/shard_map/reshape | solution.py:44
  74.2 5.1 %convolution_bitcast_fusion = f32[32,864]{1,0:T(8,128)S(1)} fusion(bf16[864,4096]{1,0:T(8,128)(2,1)} %reshape.94, bf16[32,4096]{1,0:T(8,128)(2,1)S(1)} %reshape_squeeze.3), kind=kOutput, calls=%fused_computation.32 | convolution fusion | flops 226492416 | bytes 7450624 | tf_op jit(solution)/shard_map/dot_general | solution.py:48
  79.3 0.7 pad_maximum_fusion
  80.1 12.9 %fusion.60 = f32[864,864]{1,0:T(8,128)} fusion(bf16[864,4096]{1,0:T(8,128)(2,1)} %convert_element_type.83, bf16[864,4096]{1,0:T(8,128)(2,1)} %reshape.94), kind=kOutput, calls=%fused_computation.98 | convolution fusion | flops 6115295232 | bytes 17141760 | tf_op jit(solution)/shard_map/dot_general | solution.py:59
  93.0 7.0 %copy.27 = bf16[32,27,2,16,128]{4,3,2,1,0:T(8,128)(2,1)} copy(bf16[32,27,2,16,128]{4,3,2,0,1:T(8,128)(2,1)} %get-tuple-element.4) | data formatting | bytes 14155776 | tf_op jit(solution)/shard_map/convert_element_type | solution.py:56
  100.1 11.6 %convert_element_type.86 = bf16[864,4096]{1,0:T(8,128)(2,1)} reshape(bf16[32,27,2,16,128]{4,3,2,1,0:T(8,128)(2,1)} %copy.27) | data formatting | bytes 14155776 | tf_op jit(solution)/shard_map/convert_element_type | solution.py:56
  111.6 5.0 %all-reduce.6.cloned.1.call-done = f32[32,896]{1,0:T(8,128)} async-done(((f32[32,896]{1,0:T(8,128)}), f32[32,896]{1,0:T(8,128)}) %all-reduce.6.cloned.1.call-update) | async-done | bytes 114704 | tf_op jit(solution)/shard_map/psum | solution.py:72
  116.7 13.2 %multiply_convert_fusion = bf16[864,864]{1,0:T(8,128)(2,1)} fusion(f32[864,864]{1,0:T(8,128)} %fusion.60, bf16[864,4096]{1,0:T(8,128)(2,1)} %convert_element_type.86, bf16[864,4096]{1,0:T(8,128)(2,1)} %reshape.94), kind=kOutput, calls=%fused_computation.30 | convolution fusion | flops 6117534720 | bytes 18634752 | tf_op jit(solution)/shard_map/dot_general | solution.py:60
  129.9 4.6 %reshape.96 = bf16[8,108,4,216]{3,2,1,0:T(4,128)(2,1)S(1)} reshape(bf16[864,864]{1,0:T(8,128)(2,1)} %multiply_convert_fusion) | data formatting | bytes 2985984 | tf_op jit(solution)/shard_map/reshape | solution.py:66
  134.5 2.6 %copy.28 = bf16[8,4,108,216]{2,3,1,0:T(8,128)(2,1)} copy(bf16[8,4,108,216]{3,1,2,0:T(4,128)(2,1)S(1)} %bitcast.148) | data formatting | bytes 2985984 | tf_op jit(solution)/shard_map/transpose | solution.py:67
  137.2 4.3 %fusion.1 = bf16[4,8,32,128]{3,1,2,0:T(8,128)(2,1)S(1)} fusion(bf16[32,864]{1,0:T(8,128)(2,1)S(1)} %copy-done.2, bf16[864,4096]{1,0:T(8,128)(2,1)} %reshape.94), kind=kOutput, calls=%fused_computation.31 | convolution fusion | flops 226623488 | bytes 7395328 | tf_op jit(solution)/shard_map/dot_general | solution.py:46
  141.5 0.8 copy.32
  142.3 29.0 %all-reduce.8.cloned.1.call-done = f32[32,896]{1,0:T(8,128)} async-done(((f32[32,896]{1,0:T(8,128)}), f32[32,896]{1,0:T(8,128)}) %all-reduce.8.cloned.1.call-update) | async-done | bytes 114704 | tf_op jit(solution)/shard_map/psum | solution.py:72
  171.3 1.1 fusion.54
  172.4 1.3 fusion.56
  173.7 1.4 slice.130
  175.1 52.1 %reduce-scatter.4.cloned.1.call-done = bf16[1,108,216]{1,2,0:T(8,128)(2,1)} async-done(((bf16[32,108,216]{1,2,0:T(8,128)(2,1)}), bf16[1,108,216]{1,2,0:T(8,128)(2,1)}) %reduce-scatter.4.cloned.1.call-update) | async-done | bytes 46672
  227.3 1.5 bitcast_convert_fusion
  228.7 1.6 copy.64
  (44 shorter events, 4.2 us)
Async XLA Ops:
  8.0 164.4 %copy-start = (f32[216,864]{1,0:T(8,128)S(1)}, f32[216,864]{1,0:T(8,128)}, u32[]{:S(2)}) copy-start(f32[216,864]{1,0:T(8,128)} %param.10) | copy-start | bytes 2239492
  8.0 108.6 %all-reduce.6.cloned.1.call-start = ((), (), s32[]{:S(2)}) async-start(), calls=%async_computation.1 | async-start | bytes 229376 | tf_op jit(solution)/shard_map/psum | solution.py:72
  9.1 12.0 %collective-permute-start = (bf16[1,32,1,16,128]{4,3,2,1,0:T(8,128)(2,1)S(1)}, bf16[1,32,1,16,128]{4,3,2,1,0:T(8,128)(2,1)S(1)}, u32[]{:S(2)}, u32[]{:S(2)}) collective-permute-start(bf16[1,32,1,16,128]{4,3,2,1,0:T(8,128)(2,1)S(1)} %get-tuple-element.6), channel_id=1, source_target_pairs={{0,1},{1,2},{2,3},{4,5},{5,6},{6,7},{8,9},{9,10},{10,11},{12,13},{... | collective-permute-start | bytes 393224 | tf_op jit(solution)/shard_map/ppermute | solution.py:15
  14.1 7.0 %collective-permute-start.1 = (bf16[1,32,1,16,128]{4,3,2,1,0:T(8,128)(2,1)S(1)}, bf16[1,32,1,16,128]{4,3,2,1,0:T(8,128)(2,1)S(1)}, u32[]{:S(2)}, u32[]{:S(2)}) collective-permute-start(bf16[1,32,1,16,128]{4,3,2,1,0:T(8,128)(2,1)S(1)} %get-tuple-element.7), channel_id=1, source_target_pairs={{1,0},{2,1},{3,2},{5,4},{6,5},{7,6},{9,8},{10,9},{11,10},{13,12},{... | collective-permute-start | bytes 393224 | tf_op jit(solution)/shard_map/ppermute | solution.py:17
  26.4 5.3 %copy-start.1 = (bf16[32,27,2,16,128]{4,3,2,0,1:T(8,128)(2,1)}, bf16[32,27,2,16,128]{4,3,2,0,1:T(8,128)(2,1)S(1)}, u32[]{:S(2)}) copy-start(bf16[32,27,2,16,128]{4,3,2,0,1:T(8,128)(2,1)S(1)} %fusion.49) | copy-start | bytes 21233668
  80.0 91.2 %all-reduce.8.cloned.1.call-start = ((), (), s32[]{:S(2)}) async-start(), calls=%async_computation.2 | async-start | bytes 229376 | tf_op jit(solution)/shard_map/psum | solution.py:72
  116.7 110.6 %reduce-scatter.4.cloned.1.call-start = ((), (), s32[]{:S(2)}) async-start(), calls=%async_computation.4 | async-start | bytes 1824768
  129.9 7.2 %copy-start.2 = (bf16[32,864]{1,0:T(8,128)(2,1)S(1)}, bf16[32,864]{1,0:T(8,128)(2,1)}, u32[]{:S(2)}) copy-start(bf16[32,864]{1,0:T(8,128)(2,1)} %param.8) | copy-start | bytes 165892
  134.5 36.8 %copy-start.3 = (f32[32,32]{1,0:T(8,128)S(1)}, f32[32,32]{1,0:T(8,128)}, u32[]{:S(2)}) copy-start(f32[32,32]{1,0:T(8,128)} %param.11) | copy-start | bytes 12292
  137.1 91.6 %all-reduce.10.cloned.1.call-start = ((), (), s32[]{:S(2)}) async-start(), calls=%async_computation.3 | async-start | bytes 229376 | tf_op jit(solution)/shard_map/psum | solution.py:78
Sparse Core Ops, SparseCore 0:
  80.2 36.4 all-reduce.5
  119.7 51.5 all-reduce.7
  174.3 35.3 all-reduce.9
Sparse Core Ops, SparseCore 1:
  137.2 90.0 reduce-scatter.3
